TPU v7x, 256 devices: a whole 4x4x8 slice. The times are simulated.
256 devices in a mesh: group: 16 (over y_hi, x, core), leaf: 16 (over y_lo, z).
Axes of the slice: x: 4, y: 4 (y_hi: 2, y_lo: 2; y = y_hi * 2 + y_lo), z: 8, core: 2. Of those that a mesh axis runs over, the one named last changes fastest.
Arguments:
- leaf_mass: bfloat16 [256, 512, 512], P(('group', 'leaf')), may hold values from -23 to 23, as said below
- leaf_damp: bfloat16 [256, 512, 512], P(('group', 'leaf')), may hold values from -12 to 12, as said below
- mass_coupling: bfloat16 [256, 512, 1536], P(('group', 'leaf')), may hold values from -6 to 6
- damp_coupling: bfloat16 [256, 512, 1536], P(('group', 'leaf')), may hold values from -6 to 6
- leaf_modes: bfloat16 [256, 512, 1536], P(('group', 'leaf')), may hold values from -0.15625 to 0.15625
- interface_blocks: int32 [256, 12], P(('group', 'leaf')), may hold values from 0 to 11, each once within a row
- mid_modes: bfloat16 [16, 1536, 256], P('group', 'leaf'), may hold values from -0.15625 to 0.15625
- mid_constraint: bfloat16 [16, 1536, 1024], P('group', 'leaf'), may hold values from -0.109375 to 0.109375
Outputs:
- coupling_mass: float32 [256, 512, 256], P(('group', 'leaf'))
- coupling_damp: float32 [256, 512, 256], P(('group', 'leaf'))
- modal_mass: float32 [16, 256, 1280], P('group', 'leaf')
- modal_damp: float32 [16, 256, 1280], P('group', 'leaf')
- root_mass: float32 [1024, 1024], P(('group', 'leaf'))
- root_damp: float32 [1024, 1024], P(('group', 'leaf'))
Inputs may be any that keep to these rules, and one draw needn't show every extreme that they name: `interface_blocks`: each row is a permutation of 0 to 11. `leaf_mass`: each leaf's block is symmetric. `leaf_damp`: each leaf's block is symmetric.
All inputs are finite; a program needn't handle non-finite values.
Results may differ from a plain program's by a relative error of at most 0.0049.
Values may be sent and summed in bfloat16 or wider, within the bound.
No kernel may reach another device: no remote copies, remote signals or barrier semaphores. Data moves between devices by JAX's collectives and lax.ppermute only.
A program may use at most 128 MiB of HBM per device.

v0:
```python
import jax
import jax.numpy as jnp
from jax import lax
from jax.sharding import PartitionSpec as P


def to_middle(stacked, onehot, block_count, block_size):
    rows_total, width_total = stacked.shape
    moved = jnp.einsum(
        "lbk,bj->ljk",
        stacked.reshape(rows_total, block_count, block_size),
        onehot,
        preferred_element_type=jnp.float32,
    )
    return moved.astype(jnp.bfloat16).reshape(rows_total, width_total)


def left_product(first_operand, second_operand):
    return lax.dot_general(
        first_operand, second_operand, (((0,), (0,)), ((), ())), preferred_element_type=jnp.float32
    )


def body(
    leaf_mass,
    leaf_damp,
    mass_coupling,
    damp_coupling,
    leaf_modes,
    interface_blocks,
    mid_modes,
    mid_constraint,
):
    leaf_order = leaf_mass.shape[1]
    block_count = interface_blocks.shape[1]
    sep_width = leaf_modes.shape[2]
    block_size = sep_width // block_count
    mode_count = mid_modes.shape[2]
    root_width = mid_constraint.shape[2]
    basis_width = mode_count + root_width
    leaf_count = lax.axis_size("leaf")
    group_count = lax.axis_size("group")
    onehot = (
        interface_blocks[0][:, None] == jnp.arange(block_count, dtype=jnp.int32)[None, :]
    ).astype(jnp.bfloat16)
    placed = to_middle(
        jnp.concatenate([leaf_modes[0], mass_coupling[0], damp_coupling[0]], axis=0),
        onehot,
        block_count,
        block_size,
    )
    constraint = placed[:leaf_order]
    sides = placed[leaf_order:].astype(jnp.float32)
    product = jnp.dot(
        jnp.concatenate([leaf_mass[0], leaf_damp[0]], axis=0),
        constraint,
        preferred_element_type=jnp.float32,
    )
    half_work = (0.5 * product + sides).astype(jnp.bfloat16)
    full_work = (product + sides).astype(jnp.bfloat16)
    basis_rows = jnp.concatenate([mid_modes[0], mid_constraint[0]], axis=1)
    mode_basis = lax.all_gather(basis_rows, "leaf", axis=0, tiled=True)
    left_sum = jnp.dot(constraint, mode_basis, preferred_element_type=jnp.float32)
    right_sum = jnp.dot(half_work, mode_basis, preferred_element_type=jnp.float32)
    coupling = jnp.dot(full_work, mode_basis[:, :mode_count], preferred_element_type=jnp.float32)
    left_part = left_sum.astype(jnp.bfloat16)
    right_part = right_sum.astype(jnp.bfloat16)
    right_mass = right_part[:leaf_order]
    right_damp = right_part[leaf_order:]

    def projected_rows(first_row, amount, first_col):
        left_rows = lax.dynamic_slice_in_dim(left_part, first_row, amount, 1)
        right_rows = lax.dynamic_slice_in_dim(right_part, first_row, amount, 1)
        left_cols = left_part[:, first_col:]
        mass_term = left_product(left_rows, right_mass[:, first_col:]) + left_product(
            right_rows[:leaf_order], left_cols
        )
        damp_term = left_product(left_rows, right_damp[:, first_col:]) + left_product(
            right_rows[leaf_order:], left_cols
        )
        return jnp.concatenate([mass_term, damp_term], axis=1)

    modal_part = lax.psum_scatter(
        projected_rows(jnp.int32(0), mode_count // leaf_count * lax.axis_size("leaf"), 0),
        "leaf",
        scatter_dimension=0,
        tiled=True,
    )
    root_part = lax.psum_scatter(
        projected_rows(
            jnp.int32(0) + mode_count,
            root_width // (group_count * leaf_count) * lax.axis_size(("group", "leaf")),
            mode_count,
        ),
        ("group", "leaf"),
        scatter_dimension=0,
        tiled=True,
    )
    return (
        coupling[:leaf_order][None],
        coupling[leaf_order:][None],
        modal_part[:, :basis_width][None],
        modal_part[:, basis_width:][None],
        root_part[:, :root_width],
        root_part[:, root_width:],
    )


def solution(mesh):
    return jax.shard_map(
        body,
        mesh=mesh,
        in_specs=(
            P(("group", "leaf"), None, None),
            P(("group", "leaf"), None, None),
            P(("group", "leaf"), None, None),
            P(("group", "leaf"), None, None),
            P(("group", "leaf"), None, None),
            P(("group", "leaf"), None),
            P("group", "leaf", None),
            P("group", "leaf", None),
        ),
        out_specs=(
            P(("group", "leaf"), None, None),
            P(("group", "leaf"), None, None),
            P("group", "leaf", None),
            P("group", "leaf", None),
            P(("group", "leaf"), None),
            P(("group", "leaf"), None),
        ),
        check_vma=False,
    )
```

profile of v0, /device:TPU:2, one launch (start us, length us, event | category | flops | bytes accessed | tf_op | source)
XLA Modules:
  0.0 474.5 jit_solution(488696714255146082)
XLA Ops:
  7.2 0.0 all-gather.2.cloned.1.call-start
  7.2 1.6 pad_maximum_fusion.2
  8.9 0.0 all-gather.2.cloned.1.call-update
  8.9 0.0 all-reduce.3.cloned.1.call-start
  8.9 1.7 copy.41
  10.7 0.0 copy-start.5
  10.7 3.0 copy.44
  13.7 0.7 copy.42
  14.4 0.0 copy-start.6
  14.4 3.0 copy.45
  17.5 0.7 copy.40
  18.2 0.0 copy-start.9
  18.2 3.0 copy.43
  21.2 4.6 fusion
  25.8 1.2 copy.58
  27.1 2.2 copy-done.3
  29.3 0.1 slice.74
  29.4 0.7 copy.47
  30.1 5.2 %slice_convert_fusion = f32[1024,12,128]{2,0,1:T(8,128)} fusion(bf16[1536,12,128]{2,0,1:T(8,128)(2,1)} %bitcast.34), kind=kLoop, calls=%fused_computation.13 | loop fusion | flops 1572864 | bytes 9437184 | tf_op jit(solution)/shard_map/convert_element_type | solution.py:53
  35.3 6.6 %copy.48 = f32[1024,12,128]{0,2,1:T(8,128)} copy(f32[1024,12,128]{2,0,1:T(8,128)} %slice_convert_fusion) | data formatting | bytes 12582912 | tf_op jit(solution)/shard_map/convert_element_type | solution.py:53
  41.9 6.7 %copy.49 = f32[1024,1536]{1,0:T(8,128)} copy(f32[1024,1536]{0,1:T(8,128)} %bitcast.32) | data formatting | bytes 12582912 | tf_op jit(solution)/shard_map/convert_element_type | solution.py:53
  48.6 4.5 fusion.13
  53.0 35.5 %all-gather.2.cloned.1.call-done = bf16[1536,1280]{1,0:T(8,128)(2,1)} async-done(((bf16[96,1280]{1,0:T(8,128)(2,1)}), bf16[1536,1280]{1,0:T(8,128)(2,1)}) %all-gather.2.cloned.1.call-update) | async-done | bytes 3932176 | tf_op jit(solution)/shard_map/all_gather | solution.py:62
  88.6 4.5 convolution_convert_fusion.1
  93.1 1.3 copy-done.4
  94.4 6.6 %convolution_convert_fusion = bf16[1024,1280]{1,0:T(8,128)(2,1)S(1)} fusion(bf16[1536,1280]{1,0:T(8,128)(2,1)} %all-gather.2.cloned.1.call-done, f32[1024,1536]{1,0:T(8,128)S(1)} %copy-done.2, f32[1024,1536]{1,0:T(8,128)S(1)} %copy-done.4), kind=kOutput, calls=%fused_computation.11 | convolution fusion | flops 4032561152 | bytes 19136512 | tf_op jit(solution)/shard_map/dot_general | solution.py:64
  101.0 1.3 fusion.18
  102.3 1.3 fusion.21
  103.7 1.4 convolution_add_fusion.2
  105.1 1.4 convolution_add_fusion.3
  106.5 4.1 pad_maximum_fusion
  110.6 0.0 all-reduce.3.cloned.1.call-update
  110.6 0.0 reduce-scatter.3.cloned.1.call-start
  110.7 2.0 fusion.9
  112.6 0.1 copy-done.1
  112.8 0.5 fusion.11
  113.3 0.5 convolution_add_fusion
  113.8 0.5 convolution_add_fusion.1
  114.4 1.8 pad_maximum_fusion.1
  116.1 0.0 reduce-scatter.3.cloned.1.call-update
  116.2 6.3 %fusion.7 = f32[1024,256]{1,0:T(8,128)S(1)} fusion(f32[1024,1536]{1,0:T(8,128)} %fusion.13, f32[1024,1536]{1,0:T(8,128)} %copy.49, bf16[1536,1280]{1,0:T(8,128)(2,1)} %all-gather.2.cloned.1.call-done), kind=kOutput, calls=%fused_computation.12 | convolution fusion | flops 808452096 | bytes 14417920 | tf_op jit(solution)/shard_map/dot_general | solution.py:65
  122.5 1.0 slice_bitcast_fusion
  123.5 265.2 %all-reduce.3.cloned.1.call-done = f32[1024,2048]{0,1:T(8,128)} async-done(((f32[1024,2048]{0,1:T(8,128)}), f32[1024,2048]{0,1:T(8,128)}) %all-reduce.3.cloned.1.call-update) | async-done | bytes 8388624
  388.7 1.5 fusion.38
  390.2 0.8 copy.52
  391.0 0.8 copy.51
  391.8 74.5 %reduce-scatter.3.cloned.1.call-done = f32[16,2560]{1,0:T(8,128)} async-done(((f32[256,2560]{1,0:T(8,128)}), f32[16,2560]{1,0:T(8,128)}) %reduce-scatter.3.cloned.1.call-update) | async-done | bytes 163856 | tf_op jit(solution)/shard_map/reduce_scatter | solution.py:83
  466.3 1.6 slice_bitcast_fusion.2
  (14 shorter events, 0.0 us)
Async XLA Ops:
  7.2 81.4 %all-gather.2.cloned.1.call-start = ((), (), s32[]{:S(2)}) async-start(), calls=%async_computation.1 | async-start | bytes 4177920 | tf_op jit(solution)/shard_map/all_gather | solution.py:62
  8.9 379.8 %all-reduce.3.cloned.1.call-start = ((), (), s32[]{:S(2)}) async-start(), calls=%async_computation.3 | async-start | bytes 16777216
  10.7 3.0 copy-start.5
  14.4 3.0 copy-start.6
  18.2 3.0 copy-start.9
  27.1 2.2 copy-start.3
  41.9 6.7 %copy-start.7 = (bf16[1,512,512]{2,1,0:T(8,128)(2,1)S(1)}, bf16[1,512,512]{2,1,0:T(8,128)(2,1)}, u32[]{:S(2)}) copy-start(bf16[1,512,512]{2,1,0:T(8,128)(2,1)} %param.9) | copy-start | bytes 1572868
  41.9 6.7 %copy-start.8 = (bf16[1,512,512]{2,1,0:T(8,128)(2,1)S(1)}, bf16[1,512,512]{2,1,0:T(8,128)(2,1)}, u32[]{:S(2)}) copy-start(bf16[1,512,512]{2,1,0:T(8,128)(2,1)} %param.8) | copy-start | bytes 1572868
  88.6 4.5 copy-start.2
  88.6 5.8 %copy-start.4 = (f32[1024,1536]{1,0:T(8,128)S(1)}, f32[1024,1536]{1,0:T(8,128)}, u32[]{:S(2)}) copy-start(f32[1024,1536]{1,0:T(8,128)} %fusion.13) | copy-start | bytes 18874372
  101.0 4.1 copy-start
  110.6 355.8 %reduce-scatter.3.cloned.1.call-start = ((), (), s32[]{:S(2)}) async-start(), calls=%async_computation.2 | async-start | bytes 2785280 | tf_op jit(solution)/shard_map/reduce_scatter | solution.py:83
  110.6 2.1 copy-start.1
Sparse Core Ops, SparseCore 0:
  10.3 78.1 all-gather.1
  110.7 277.9 all-reduce.2
  391.3 75.0 reduce-scatter.2
where the time goes:
time: 475 us; the launch traced here: 474 us
  waiting for transfers between devices  375 us (79%)
  local copies, waits for them, and re-layouts  36.9 us (8%)
  matrix products  35.6 us (7%)
  between operations  13.9 us (3%)
  other arithmetic  12.6 us (3%)
    unnamed x4, waiting for transfers between devices  265 us
    reduce_scatter x1, waiting for transfers between devices, body(): lax.psum_scatter(projected_rows(jnp.int32(0), mode_count // leaf_count *...  74.5 us
    all_gather x1, waiting for transfers between devices, body(): mode_basis = lax.all_gather(basis_rows, 'leaf', axis=0, tiled=True)  35.5 us
    convert_element_type x2, local copies, waits for them, and re-layouts, body(): sides = placed[leaf_order:].astype(jnp.float32)  13.3 us
  transfers between devices with their start and end apart: 3, of which 3 were waited for; matrix products, arithmetic and copies ran while one was open for 12% of the time, Pallas kernels for 0%

commit v1 on v0

--- a/solution.py
+++ b/solution.py
@@ -59,7 +59,9 @@
     half_work = (0.5 * product + sides).astype(jnp.bfloat16)
     full_work = (product + sides).astype(jnp.bfloat16)
     basis_rows = jnp.concatenate([mid_modes[0], mid_constraint[0]], axis=1)
-    mode_basis = lax.all_gather(basis_rows, "leaf", axis=0, tiled=True)
+    mode_basis = jnp.concatenate(
+        lax.all_to_all(jnp.stack([basis_rows] * lax.axis_size("leaf")), "leaf", 0, 0), axis=0
+    )
     left_sum = jnp.dot(constraint, mode_basis, preferred_element_type=jnp.float32)
     right_sum = jnp.dot(half_work, mode_basis, preferred_element_type=jnp.float32)
     coupling = jnp.dot(full_work, mode_basis[:, :mode_count], preferred_element_type=jnp.float32)

time: 475 us -> 431 us (0.907)
  waiting for transfers between devices: 375 us -> 320 us
  starting transfers between devices: 0.12 us -> 9.84 us
    reduce_scatter x1, waiting for transfers between devices: 74.5 us -> 0.01 us  [body(): lax.psum_scatter(projected_rows(jnp.int32(0), mode_count // leaf_count *...]
    all_to_all x0 -> x1, waiting for transfers between devices: none -> 46.5 us  [body(): lax.all_to_all(jnp.stack([basis_rows] * lax.axis_size('leaf')), 'leaf', 0...]
    all_gather x1 -> x0, waiting for transfers between devices: 35.5 us -> none  [body(): mode_basis = lax.all_gather(basis_rows, 'leaf', axis=0, tiled=True)]
    all_to_all x0 -> x1, starting transfers between devices: none -> 9.76 us  [body(): lax.all_to_all(jnp.stack([basis_rows] * lax.axis_size('leaf')), 'leaf', 0...]
    unnamed x4 -> x3, waiting for transfers between devices: 265 us -> 273 us
  transfers between devices with their start and end apart: 3 -> 3, of which waited for: 3 -> 2; matrix products, arithmetic and copies ran while one was open for 12% -> 13% of each run, Pallas kernels for 0% -> 0%
where the time goes in v1:
time: 431 us; the launch traced here: 430 us
  waiting for transfers between devices  320 us (74%)
  local copies, waits for them, and re-layouts  38.1 us (9%)
  matrix products  35 us (8%)
  between operations  15.7 us (4%)
  other arithmetic  11.9 us (3%)
  starting transfers between devices  9.84 us (2%)
    unnamed x3, waiting for transfers between devices  273 us
    all_to_all x1, waiting for transfers between devices, body(): lax.all_to_all(jnp.stack([basis_rows] * lax.axis_size('leaf')), 'leaf', 0...  46.5 us
    convert_element_type x2, local copies, waits for them, and re-layouts, body(): sides = placed[leaf_order:].astype(jnp.float32)  13.2 us
    all_to_all x1, starting transfers between devices, body(): lax.all_to_all(jnp.stack([basis_rows] * lax.axis_size('leaf')), 'leaf', 0...  9.76 us
    concatenate x3, local copies, waits for them, and re-layouts, body(): jnp.concatenate([leaf_modes[0], mass_coupling[0], damp_coupling[0]], axis=0)  9.09 us
    dot_general x8, matrix products, left_product(): lax.dot_general(first_operand, second_operand, (((0,), (0,)), ((), ())),...  9.03 us
  transfers between devices with their start and end apart: 3, of which 2 were waited for; matrix products, arithmetic and copies ran while one was open for 13% of the time, Pallas kernels for 0%

profile of v1, /device:TPU:2, one launch (start us, length us, event | category | flops | bytes accessed | tf_op | source)
XLA Modules:
  0.0 430.3 jit_solution(2127604607598748169)
XLA Ops:
  8.0 0.9 pad_maximum_fusion.2
  8.9 2.3 stack.2
  11.2 9.8 %all-to-all-start = ((bf16[16,96,1280]{2,1,0:T(8,128)(2,1)}), bf16[16,96,1280]{2,1,0:T(8,128)(2,1)}, u32[]{:S(2)}, u32[]{:S(2)}) async-start(bf16[16,96,1280]{2,1,0:T(8,128)(2,1)} %stack.2), calls=%async_computation | async-start | bytes 7864320 | tf_op jit(solution)/shard_map/all_to_all | solution.py:63
  21.0 0.0 all-reduce.3.cloned.1.call-start
  21.0 0.7 copy.41
  21.7 0.0 copy-start.6
  21.8 3.0 copy.44
  24.8 0.7 copy.42
  25.5 0.0 copy-start.7
  25.5 3.0 copy.45
  28.5 0.7 copy.40
  29.3 0.0 copy-start.10
  29.3 3.0 copy.43
  32.3 4.6 %fusion = bf16[12,1536,128]{2,0,1:T(8,128)(2,1)S(1)} fusion(bf16[512,12,128]{2,1,0:T(8,128)(2,1)} %copy.45, bf16[512,12,128]{2,1,0:T(8,128)(2,1)} %copy.44, bf16[512,12,128]{2,1,0:T(8,128)(2,1)} %copy.43, s32[12]{0:T(128)S(1)} %bitcast.45), kind=kOutput, calls=%fused_computation.2 | convolution fusion | flops 70779024 | bytes 9437232 | tf_op jit(solution)/shard_map/lbk,bj->ljk/dot_general | solution.py:9
  36.9 1.2 copy.58
  38.2 2.2 copy-done.3
  40.4 0.1 slice.74
  40.5 0.7 copy.47
  41.2 5.1 %slice_convert_fusion = f32[1024,12,128]{2,0,1:T(8,128)} fusion(bf16[1536,12,128]{2,0,1:T(8,128)(2,1)} %bitcast.35), kind=kLoop, calls=%fused_computation.13 | loop fusion | flops 1572864 | bytes 9437184 | tf_op jit(solution)/shard_map/convert_element_type | solution.py:53
  46.3 6.6 %copy.48 = f32[1024,12,128]{0,2,1:T(8,128)} copy(f32[1024,12,128]{2,0,1:T(8,128)} %slice_convert_fusion) | data formatting | bytes 12582912 | tf_op jit(solution)/shard_map/convert_element_type | solution.py:53
  52.9 6.7 %copy.49 = f32[1024,1536]{1,0:T(8,128)} copy(f32[1024,1536]{0,1:T(8,128)} %bitcast.33) | data formatting | bytes 12582912 | tf_op jit(solution)/shard_map/convert_element_type | solution.py:53
  59.6 0.0 copy-done.9
  59.6 4.5 %fusion.13 = f32[1024,1536]{1,0:T(8,128)} fusion(bf16[512,1536]{0,1:T(8,128)(2,1)S(1)} %bitcast.39, bf16[512,512]{1,0:T(8,128)(2,1)S(1)} %bitcast.43, bf16[512,512]{1,0:T(8,128)(2,1)S(1)} %bitcast.44), kind=kOutput, calls=%fused_computation.25 | convolution fusion | flops 1612709888 | bytes 8912896 | tf_op jit(solution)/shard_map/dot_general | solution.py:54
  64.0 46.5 %all-to-all-done = bf16[16,96,1280]{2,1,0:T(8,128)(2,1)} async-done(((bf16[16,96,1280]{2,1,0:T(8,128)(2,1)}), bf16[16,96,1280]{2,1,0:T(8,128)(2,1)}, u32[]{:S(2)}, u32[]{:S(2)}) %all-to-all-start) | async-done | bytes 3932192 | tf_op jit(solution)/shard_map/all_to_all | solution.py:63
  110.6 4.5 %convolution_convert_fusion.1 = bf16[512,1280]{1,0:T(8,128)(2,1)S(1)} fusion(bf16[512,1536]{0,1:T(8,128)(2,1)S(1)} %bitcast.40, bf16[1536,1280]{1,0:T(8,128)(2,1)} %bitcast.12), kind=kOutput, calls=%fused_computation.15 | convolution fusion | flops 2013921280 | bytes 6815744 | tf_op jit(solution)/shard_map/dot_general | solution.py:65
  115.1 1.3 copy-done.4
  116.4 6.6 %convolution_convert_fusion = bf16[1024,1280]{1,0:T(8,128)(2,1)S(1)} fusion(bf16[1536,1280]{1,0:T(8,128)(2,1)} %bitcast.12, f32[1024,1536]{1,0:T(8,128)S(1)} %copy-done.2, f32[1024,1536]{1,0:T(8,128)S(1)} %copy-done.4), kind=kOutput, calls=%fused_computation.11 | convolution fusion | flops 4032561152 | bytes 19136512 | tf_op jit(solution)/shard_map/dot_general | solution.py:66
  123.0 1.3 fusion.18
  124.3 1.3 fusion.21
  125.6 1.4 convolution_add_fusion.2
  127.1 1.4 convolution_add_fusion.3
  128.5 4.1 pad_maximum_fusion
  132.6 0.0 all-reduce.3.cloned.1.call-update
  132.6 0.0 reduce-scatter.3.cloned.1.call-start
  132.6 2.0 fusion.9
  134.6 0.1 copy-done.1
  134.8 0.5 fusion.11
  135.3 0.5 convolution_add_fusion
  135.8 0.5 convolution_add_fusion.1
  136.4 1.8 pad_maximum_fusion.1
  138.1 0.0 reduce-scatter.3.cloned.1.call-update
  138.2 5.7 %fusion.7 = f32[1024,256]{1,0:T(8,128)S(1)} fusion(f32[1024,1536]{1,0:T(8,128)} %fusion.13, f32[1024,1536]{1,0:T(8,128)} %copy.49, bf16[1536,1280]{1,0:T(8,128)(2,1)} %bitcast.12), kind=kOutput, calls=%fused_computation.12 | convolution fusion | flops 808452096 | bytes 14417920 | tf_op jit(solution)/shard_map/dot_general | solution.py:67
  143.9 1.0 slice_bitcast_fusion
  144.9 273.2 %all-reduce.3.cloned.1.call-done = f32[1024,2048]{0,1:T(8,128)} async-done(((f32[1024,2048]{0,1:T(8,128)}), f32[1024,2048]{0,1:T(8,128)}) %all-reduce.3.cloned.1.call-update) | async-done | bytes 8388624
  418.1 1.5 fusion.38
  419.6 0.8 copy.52
  420.4 0.8 copy.51
  421.2 1.6 slice_bitcast_fusion.2
  (16 shorter events, 0.0 us)
Async XLA Ops:
  11.2 9.8 %copy-start.5 = (bf16[1,512,1536]{2,1,0:T(8,128)(2,1)S(1)}, bf16[1,512,1536]{2,1,0:T(8,128)(2,1)}, u32[]{:S(2)}) copy-start(bf16[1,512,1536]{2,1,0:T(8,128)(2,1)} %param.10) | copy-start | bytes 4718596
  11.2 99.4 %all-to-all-start = ((bf16[16,96,1280]{2,1,0:T(8,128)(2,1)}), bf16[16,96,1280]{2,1,0:T(8,128)(2,1)}, u32[]{:S(2)}, u32[]{:S(2)}) async-start(bf16[16,96,1280]{2,1,0:T(8,128)(2,1)} %stack.2), calls=%async_computation | async-start | bytes 7864320 | tf_op jit(solution)/shard_map/all_to_all | solution.py:63
  21.0 397.1 %all-reduce.3.cloned.1.call-start = ((), (), s32[]{:S(2)}) async-start(), calls=%async_computation.3 | async-start | bytes 16777216
  21.7 3.0 copy-start.6
  25.5 3.0 copy-start.7
  29.3 3.0 copy-start.10
  38.2 2.2 copy-start.3
  52.9 6.7 %copy-start.8 = (bf16[1,512,512]{2,1,0:T(8,128)(2,1)S(1)}, bf16[1,512,512]{2,1,0:T(8,128)(2,1)}, u32[]{:S(2)}) copy-start(bf16[1,512,512]{2,1,0:T(8,128)(2,1)} %param.9) | copy-start | bytes 1572868
  52.9 6.7 %copy-start.9 = (bf16[1,512,512]{2,1,0:T(8,128)(2,1)S(1)}, bf16[1,512,512]{2,1,0:T(8,128)(2,1)}, u32[]{:S(2)}) copy-start(bf16[1,512,512]{2,1,0:T(8,128)(2,1)} %param.8) | copy-start | bytes 1572868
  110.6 4.5 %copy-start.2 = (f32[1024,1536]{1,0:T(8,128)S(1)}, f32[1024,1536]{1,0:T(8,128)}, u32[]{:S(2)}) copy-start(f32[1024,1536]{1,0:T(8,128)} %copy.49) | copy-start | bytes 18874372
  110.6 5.8 %copy-start.4 = (f32[1024,1536]{1,0:T(8,128)S(1)}, f32[1024,1536]{1,0:T(8,128)}, u32[]{:S(2)}) copy-start(f32[1024,1536]{1,0:T(8,128)} %fusion.13) | copy-start | bytes 18874372
  123.0 4.1 copy-start
  132.6 288.6 %reduce-scatter.3.cloned.1.call-start = ((), (), s32[]{:S(2)}) async-start(), calls=%async_computation.2 | async-start | bytes 2785280 | tf_op jit(solution)/shard_map/reduce_scatter | solution.py:85
  132.6 2.1 copy-start.1
Sparse Core Ops, SparseCore 0:
  132.7 285.3 all-reduce.2
Sparse Core Ops, SparseCore 1:
  138.2 79.0 reduce-scatter.2
